TPU v7x, 256 devices: a whole 4x4x8 slice. The times are simulated.
256 devices in a mesh: section: 2 (over y_hi), grp: 4 (over x), tok: 32 (over y_lo, z, core).
Axes of the slice: x: 4, y: 4 (y_hi: 2, y_lo: 2; y = y_hi * 2 + y_lo), z: 8, core: 2. Of those that a mesh axis runs over, the one named last changes fastest.
Arguments:
- image_in: bfloat16 [2, 4, 128, 3072], P('section', 'grp', 'tok'), may hold values from -1.5 to 1.5
- text_in: bfloat16 [2, 4, 512, 3072], P('section', 'grp', 'tok'), may hold values from -1.5 to 1.5
- text_length: int32 [4], P('grp'), may hold values from 256 to 512, as said below
- entry_order: int32 [4, 4], P('grp'), may hold values from 0 to 3, as said below
- step_index: int32 [4, 4], P('grp'), may hold values from 0 to 3
- image_modulation: bfloat16 [2, 4, 18432], P('section'), may hold values from -3 to 3
- text_modulation: bfloat16 [2, 4, 9216], P('section'), may hold values from -3 to 3
- image_to_heads: bfloat16 [2, 3072, 9216], P('section', None, 'tok'), may hold values from -0.109375 to 0.109375
- text_to_heads: bfloat16 [2, 3072, 9216], P('section', None, 'tok'), may hold values from -0.109375 to 0.109375
- head_gain: float32 [2, 4, 128], P('section'), may hold values from 0.5 to 2
- image_from_heads: bfloat16 [2, 3072, 3072], P('section', None, 'tok'), may hold values from -0.109375 to 0.109375
- text_from_heads: bfloat16 [2, 3072, 3072], P('section', None, 'tok'), may hold values from -0.109375 to 0.109375
- image_up: bfloat16 [2, 3072, 12288], P('section', None, 'tok'), may hold values from -0.109375 to 0.109375
- image_down: bfloat16 [2, 12288, 3072], P('section', 'tok'), may hold values from -0.0546875 to 0.0546875
- stale_cache: bfloat16 [2, 4, 512, 6144], P('section', 'grp', 'tok'), may hold values from -400 to 400
- final_modulation: bfloat16 [4, 6144], replicated, may hold values from -3 to 3
- final_weight: bfloat16 [3072, 64], P(None, 'section'), may hold values from -0.109375 to 0.109375
- latents: float32 [4, 128, 64], P('grp', 'tok', 'section'), may hold values from -6 to 6
Outputs:
- image_handoff: bfloat16 [2, 4, 128, 3072], P('section', 'grp', 'tok')
- text_handoff: bfloat16 [2, 4, 512, 3072], P('section', 'grp', 'tok')
- fresh_cache: bfloat16 [2, 4, 512, 6144], P('section', 'grp', 'tok')
- latents_next: float32 [4, 128, 64], P('grp', 'tok', 'section')
Inputs may be any that keep to these rules, and one draw needn't show every extreme that they name: `text_length`: valid text tokens of each request; some request has exactly 512. `entry_order`: each row is a permutation of the 4 patch numbers.
All inputs are finite; a program needn't handle non-finite values.
Results may differ from a plain program's by a relative error of at most 0.023.
The roundings to bfloat16 on the way count: a program that leaves them out, or rounds other values in their place, can miss the bound.
Values may be sent and summed in bfloat16 or wider, within the bound.
No kernel may reach another device: no remote copies, remote signals or barrier semaphores. Data moves between devices by JAX's collectives and lax.ppermute only.
A program may use at most 128 MiB of HBM per device.

v0:
```python
import jax
import jax.numpy as jnp
from jax import lax
from jax.sharding import PartitionSpec as P

HDIM = 128
TSTEPS = 4
eps = 1e-06
masked_score = -1e30


def from_behind(block, axis, distance):
    devices = range(lax.axis_size(axis))
    route = [((i - distance) % len(devices), i) for i in devices]
    return lax.ppermute(block, axis, route)


def layer_norm(field):
    mean = jnp.mean(field, axis=-1, keepdims=True)
    centred = field - mean
    spread = jnp.mean(centred * centred, axis=-1, keepdims=True)
    return centred * lax.rsqrt(spread + eps)


def modulate(field, shift, scale):
    return layer_norm(field) * (1.0 + scale) + shift


def head_norm(field, gain):
    height, width = field.shape
    shaped = field.reshape(height, width // HDIM, HDIM)
    power = jnp.mean(shaped * shaped, axis=-1, keepdims=True)
    return (shaped * lax.rsqrt(power + eps) * gain).reshape(height, width)


def attend(carry, queries, piece, valid):
    highest, total, mixed = carry
    height, width = queries.shape
    heads = width // HDIM
    keys = piece[:, :width].reshape(-1, heads, HDIM)
    values = piece[:, width:].reshape(-1, heads, HDIM)
    scores = jnp.einsum(
        "qhd,khd->qhk",
        queries.reshape(height, heads, HDIM),
        keys,
        preferred_element_type=jnp.float32,
    ) * HDIM ** (-0.5)
    scores = jnp.where(valid[None, None, :], scores, masked_score)
    new_high = jnp.maximum(highest, jnp.max(scores, axis=-1))
    expo = jnp.where(valid[None, None, :], jnp.exp(scores - new_high[..., None]), 0.0)
    keep = jnp.exp(highest - new_high)
    total = total * keep + jnp.sum(expo, axis=-1)
    mixed = mixed * keep[..., None] + jnp.einsum(
        "qhk,khd->qhd", expo.astype(jnp.bfloat16), values, preferred_element_type=jnp.float32
    )
    return (new_high, total, mixed)


def empty_carry(height, heads):
    return (
        jnp.full((height, heads), masked_score, jnp.float32),
        jnp.zeros((height, heads), jnp.float32),
        jnp.zeros((height, heads, HDIM), jnp.float32),
    )


def shards(
    image_in,
    text_in,
    text_length,
    entry_order,
    step_index,
    image_modulation,
    text_modulation,
    image_to_heads,
    text_to_heads,
    head_gain,
    image_from_heads,
    text_from_heads,
    image_up,
    image_down,
    stale_cache,
    final_modulation,
    final_weight,
    latents,
):
    section = lax.axis_index("section")
    last_section = lax.axis_size("section") - 1
    position = lax.axis_index("tok")
    image_x = image_in[0, 0].astype(jnp.float32)
    text_x = text_in[0, 0].astype(jnp.float32)
    image_rows = image_x.shape[0]
    width = image_x.shape[1]
    heads = width // HDIM
    patch = lax.dynamic_index_in_dim(entry_order[0], section, 0, False)
    step_now = lax.dynamic_index_in_dim(step_index[0], patch, 0, False)
    modul = (
        lax.dynamic_index_in_dim(image_modulation[0], step_now, 0, False)
        .astype(jnp.float32)
        .reshape(6, width)
    )
    text_mod = (
        lax.dynamic_index_in_dim(text_modulation[0], step_now, 0, False)
        .astype(jnp.float32)
        .reshape(3, width)
    )
    image_normed = modulate(image_x, modul[0], modul[1]).astype(jnp.bfloat16)
    text_normed = modulate(text_x, text_mod[0], text_mod[1]).astype(jnp.bfloat16)
    every_image, every_text = (
        lax.all_gather(image_normed, "tok", axis=0, tiled=True),
        lax.all_gather(text_normed, "tok", axis=0, tiled=True),
    )
    image_cols = jnp.dot(every_image, image_to_heads[0], preferred_element_type=jnp.float32).astype(
        jnp.bfloat16
    )
    text_cols = jnp.dot(every_text, text_to_heads[0], preferred_element_type=jnp.float32).astype(
        jnp.bfloat16
    )
    image_proj, text_proj = (
        lax.all_to_all(image_cols, "tok", split_axis=0, concat_axis=1, tiled=True),
        lax.all_to_all(text_cols, "tok", split_axis=0, concat_axis=1, tiled=True),
    )
    gains = head_gain[0]
    image_query = head_norm(image_proj[:, :width].astype(jnp.float32), gains[0]).astype(
        jnp.bfloat16
    )
    image_key = head_norm(image_proj[:, width : 2 * width].astype(jnp.float32), gains[1]).astype(
        jnp.bfloat16
    )
    text_query = head_norm(text_proj[:, :width].astype(jnp.float32), gains[2]).astype(jnp.bfloat16)
    text_key = head_norm(text_proj[:, width : 2 * width].astype(jnp.float32), gains[3]).astype(
        jnp.bfloat16
    )
    fresh_image = jnp.concatenate([image_key, image_proj[:, 2 * width :]], axis=1)
    fresh_text = jnp.concatenate([text_key, text_proj[:, 2 * width :]], axis=1)
    queries = jnp.concatenate([image_query, text_query], axis=0)
    query_rows = queries.shape[0]
    patch_rows = lax.all_gather(fresh_image, "tok", axis=0, tiled=True)
    stale = stale_cache[0, 0]
    cache_rows = stale.shape[0]
    patch_len = patch_rows.shape[0]
    first_row = position * cache_rows
    begin = patch * patch_len
    offset = jnp.clip(first_row - begin, 0, patch_len - cache_rows)
    window = lax.dynamic_slice_in_dim(patch_rows, offset, cache_rows, 0)
    inside = jnp.logical_and(first_row >= begin, first_row < begin + patch_len)
    current = jnp.where(inside, window, stale)
    text_count = text_length[0]
    piece = lax.all_gather(current, "tok", axis=0, tiled=True)
    carry = attend(
        empty_carry(query_rows, heads), queries, piece, jnp.ones((piece.shape[0],), bool)
    )
    piece = lax.all_gather(fresh_text, "tok", axis=0, tiled=True)
    where_text = jnp.arange(piece.shape[0], dtype=jnp.int32)
    highest, total, mixed = attend(carry, queries, piece, where_text < text_count)
    attended = (mixed / total[..., None]).reshape(query_rows, width).astype(jnp.bfloat16)
    every_image_att, every_text_att = (
        lax.all_gather(attended[:image_rows], "tok", axis=0, tiled=True),
        lax.all_gather(attended[image_rows:], "tok", axis=0, tiled=True),
    )
    image_back_cols = jnp.dot(
        every_image_att, image_from_heads[0], preferred_element_type=jnp.float32
    ).astype(jnp.bfloat16)
    text_back_cols = jnp.dot(
        every_text_att, text_from_heads[0], preferred_element_type=jnp.float32
    ).astype(jnp.bfloat16)
    image_back, text_back = (
        lax.all_to_all(image_back_cols, "tok", split_axis=0, concat_axis=1, tiled=True),
        lax.all_to_all(text_back_cols, "tok", split_axis=0, concat_axis=1, tiled=True),
    )
    image_mid = image_x + modul[2] * image_back.astype(jnp.float32)
    text_out = (text_x + text_mod[2] * text_back.astype(jnp.float32)).astype(jnp.bfloat16)
    mlp_normed = modulate(image_mid, modul[3], modul[4]).astype(jnp.bfloat16)
    up_weight = image_up[0]
    down_weight = image_down[0]
    hidden = jax.nn.gelu(
        jnp.dot(
            lax.all_gather(mlp_normed, "tok", axis=0, tiled=True),
            up_weight,
            preferred_element_type=jnp.float32,
        ),
        approximate=True,
    ).astype(jnp.bfloat16)
    reduced = lax.psum_scatter(
        jnp.dot(hidden, down_weight, preferred_element_type=jnp.float32),
        "tok",
        scatter_dimension=0,
        tiled=True,
    )
    image_out = (image_mid + modul[5] * reduced).astype(jnp.bfloat16)
    joined = from_behind(jnp.concatenate([image_out, text_out], axis=0), "section", 1)
    image_next = joined[:image_rows]
    text_next = joined[image_rows:]
    final_source = jnp.where(section == last_section, image_out, image_next)
    patch_last = entry_order[0, last_section]
    step_last = lax.dynamic_index_in_dim(step_index[0], patch_last, 0, False)
    final_mod = (
        lax.dynamic_index_in_dim(final_modulation, step_last, 0, False)
        .astype(jnp.float32)
        .reshape(2, width)
    )
    normed = modulate(final_source.astype(jnp.float32), final_mod[0], final_mod[1]).astype(
        jnp.bfloat16
    )
    velocity = jnp.dot(normed, final_weight, preferred_element_type=jnp.float32)
    latents_next = latents[0] + -1.0 / TSTEPS * velocity
    return (image_next[None, None], text_next[None, None], current[None, None], latents_next[None])


def solution(mesh):
    placed = (
        P("section", "grp", "tok", None),
        P("section", "grp", "tok", None),
        P("grp"),
        P("grp", None),
        P("grp", None),
        P("section", None, None),
        P("section", None, None),
        P("section", None, "tok"),
        P("section", None, "tok"),
        P("section", None, None),
        P("section", None, "tok"),
        P("section", None, "tok"),
        P("section", None, "tok"),
        P("section", "tok", None),
        P("section", "grp", "tok", None),
        P(),
        P(None, "section"),
        P("grp", "tok", "section"),
    )
    return jax.shard_map(
        shards,
        mesh=mesh,
        in_specs=placed,
        out_specs=(
            P("section", "grp", "tok", None),
            P("section", "grp", "tok", None),
            P("section", "grp", "tok", None),
            P("grp", "tok", "section"),
        ),
        check_vma=False,
    )
```

profile of v0, /device:TPU:1, one launch (start us, length us, event | category | flops | bytes accessed | tf_op | source)
XLA Modules:
  0.0 711.8 jit_solution(14484903372511090327)
XLA Ops:
  7.2 1.5 fusion.114
  12.5 1.3 constant_dynamic-slice_fusion
  15.8 1.0 dynamic-slice_convert_fusion
  16.8 0.6 fusion.112
  17.4 0.9 convert_reduce_fusion.2
  18.3 0.9 fusion.80
  19.2 0.8 fusion.94
  20.1 40.7 %all-gather = bf16[32,4,3072]{2,1,0:T(4,128)(2,1)S(1)} all-gather(bf16[1,4,3072]{2,1,0:T(4,128)(2,1)S(1)} %fusion.94), channel_id=1, replica_groups=mesh['section'=2,'grp'=4,'tok'=32] {'tok'}, dimensions={0}, use_global_device_ids=true | all-gather | bytes 811008 | tf_op jit(solution)/shard_map/all_gather | solution.py:110
  60.8 1.1 reshape.264
  61.9 2.4 fusion.19
  64.4 0.7 all_to_all.48
  65.1 3.7 all-to-all-start
  68.8 8.5 %all-to-all-done = bf16[32,4,288]{2,1,0:T(4,128)(2,1)S(1)} async-done(((bf16[32,4,288]{2,1,0:T(4,128)(2,1)}), bf16[32,4,288]{2,1,0:T(4,128)(2,1)S(1)}, u32[]{:S(2)}, u32[]{:S(2)}) %all-to-all-start) | async-done | bytes 73760 | tf_op jit(solution)/shard_map/all_to_all | solution.py:120
  77.8 0.7 fusion.93
  78.5 0.6 maximum_bitcast_fusion
  79.4 0.2 fusion.40
  79.6 0.6 fusion.113
  80.3 0.7 fusion.43
  81.7 59.4 %all-gather.18.cloned.1.call-done = bf16[32,4,6144]{2,1,0:T(4,128)(2,1)} async-done(((bf16[1,4,6144]{2,1,0:T(4,128)(2,1)}), bf16[32,4,6144]{2,1,0:T(4,128)(2,1)}) %all-gather.18.cloned.1.call-update) | async-done | bytes 1572880 | tf_op jit(solution)/shard_map/all_gather | solution.py:138
  141.1 3.7 reshape.266
  144.8 1.7 bitcast_select_fusion
  146.5 62.8 %all-gather.12.cloned.1.call-done = bf16[512,3072]{1,0:T(8,128)(2,1)} async-done(((bf16[16,3072]{1,0:T(8,128)(2,1)}), bf16[512,3072]{1,0:T(8,128)(2,1)}) %all-gather.12.cloned.1.call-update) | async-done | bytes 3145744 | tf_op jit(solution)/shard_map/all_gather | solution.py:111
  209.3 3.5 fusion.11
  212.9 0.9 copy.62
  213.8 6.6 all-to-all-start.1
  220.5 16.5 %all-to-all-done.1 = bf16[32,16,288]{2,1,0:T(8,128)(2,1)S(1)} async-done(((bf16[32,16,288]{2,1,0:T(8,128)(2,1)}), bf16[32,16,288]{2,1,0:T(8,128)(2,1)S(1)}, u32[]{:S(2)}, u32[]{:S(2)}) %all-to-all-start.1) | async-done | bytes 294944 | tf_op jit(solution)/shard_map/all_to_all | solution.py:121
  237.0 0.5 all_to_all.55
  238.3 0.7 pad_maximum_fusion
  239.7 0.7 copy.105
  240.4 45.5 %all-gather.10.cloned.1.call-done = bf16[512,6144]{1,0:T(8,128)(2,1)} async-done(((bf16[16,6144]{1,0:T(8,128)(2,1)}), bf16[512,6144]{1,0:T(8,128)(2,1)}) %all-gather.10.cloned.1.call-update) | async-done | bytes 6291472 | tf_op jit(solution)/shard_map/all_gather | solution.py:149
  285.8 5.9 fusion.111
  291.7 4.8 copy.82
  296.5 4.7 copy.81
  301.2 2.6 fusion.115
  303.7 53.0 %all-gather.14.cloned.1.call-done = bf16[512,6144]{1,0:T(8,128)(2,1)} async-done(((bf16[16,6144]{1,0:T(8,128)(2,1)}), bf16[512,6144]{1,0:T(8,128)(2,1)}) %all-gather.14.cloned.1.call-update) | async-done | bytes 6291472 | tf_op jit(solution)/shard_map/all_gather | solution.py:153
  356.7 6.0 fusion.110
  362.7 4.7 copy.68
  367.4 4.7 copy.70
  372.0 2.7 fusion.116
  374.8 0.4 fusion.26
  375.1 0.4 fusion.24
  375.6 1.0 fusion.17
  376.5 0.9 copy-done.2
  377.4 1.0 fusion.18
  378.4 0.7 copy_bitcast_fusion
  379.2 0.2 all-reduce.3.cloned.1.call-start
  379.4 34.4 %all-gather.2 = bf16[32,4,3072]{2,1,0:T(4,128)(2,1)S(1)} all-gather(bf16[1,4,3072]{2,1,0:T(4,128)(2,1)S(1)} %slice_bitcast_fusion.2), channel_id=1, replica_groups=mesh['section'=2,'grp'=4,'tok'=32] {'tok'}, dimensions={0}, use_global_device_ids=true | all-gather | bytes 811008 | tf_op jit(solution)/shard_map/all_gather | solution.py:158
  413.9 1.1 reshape.268
  414.9 1.7 convolution_convert_fusion.1
  416.7 12.0 %all_to_all.64 = bf16[32,4,96]{2,1,0:T(4,128)(2,1)S(1)} all-to-all(bf16[32,4,96]{2,1,0:T(4,128)(2,1)S(1)} %bitcast.220), channel_id=1, replica_groups=mesh['section'=2,'grp'=4,'tok'=32] {'tok'}, dimensions={0} | all-to-all | bytes 49152 | tf_op jit(solution)/shard_map/all_to_all | solution.py:168
  429.3 36.7 %all-gather.3 = bf16[32,4,3072]{2,1,0:T(4,128)(2,1)} all-gather(bf16[1,4,3072]{2,1,0:T(4,128)(2,1)S(1)} %fusion.92), channel_id=1, replica_groups=mesh['section'=2,'grp'=4,'tok'=32] {'tok'}, dimensions={0}, use_global_device_ids=true | all-gather | bytes 811008 | tf_op jit(solution)/shard_map/all_gather | solution.py:178
  466.0 1.6 reshape.270
  467.6 4.0 fusion
  473.0 0.6 dynamic-slice.5
  475.0 3.0 convolution_convert_fusion
  478.0 0.8 copy.75
  478.8 3.7 all-to-all-start.3
  482.5 212.0 %all-reduce.3.cloned.1.call-done = f32[128,3072]{1,0:T(8,128)} async-done(((f32[128,3072]{1,0:T(8,128)}), f32[128,3072]{1,0:T(8,128)}) %all-reduce.3.cloned.1.call-update) | async-done | bytes 1572880
  694.5 0.9 fusion.91
  695.8 2.5 collective-permute-start
  698.4 4.1 collective-permute-done
  702.9 0.8 fusion.23
  703.7 0.6 slice_bitcast_fusion.3
  704.3 0.7 slice_bitcast_fusion
  (105 shorter events, 3.5 us)
Async XLA Ops:
  7.2 460.4 %copy-start = (bf16[1,384,3072]{2,1,0:T(8,128)(2,1)S(1)}, bf16[1,384,3072]{2,1,0:T(8,128)(2,1)}, u32[]{:S(2)}) copy-start(bf16[1,384,3072]{2,1,0:T(8,128)(2,1)} %param.31) | copy-start | bytes 7077892
  61.9 6.9 copy-start.15
  61.9 17.3 %copy-start.3 = (bf16[1,1,16,3072]{3,2,1,0:T(8,128)(2,1)S(1)}, bf16[1,1,16,3072]{3,2,1,0:T(8,128)(2,1)}, u32[]{:S(2)}) copy-start(bf16[1,1,16,3072]{3,2,1,0:T(8,128)(2,1)} %param.19) | copy-start | bytes 294916
  61.9 17.7 %copy-start.13 = (bf16[1,4,9216]{2,1,0:T(4,128)(2,1)S(1)}, bf16[1,4,9216]{2,1,0:T(4,128)(2,1)}, u32[]{:S(2)}) copy-start(bf16[1,4,9216]{2,1,0:T(4,128)(2,1)} %param.24) | copy-start | bytes 221188
  65.1 12.2 %all-to-all-start = ((bf16[32,4,288]{2,1,0:T(4,128)(2,1)}), bf16[32,4,288]{2,1,0:T(4,128)(2,1)S(1)}, u32[]{:S(2)}, u32[]{:S(2)}) async-start(bf16[32,4,288]{2,1,0:T(4,128)(2,1)} %all_to_all.48), calls=%async_computation | async-start | bytes 196608 | tf_op jit(solution)/shard_map/all_to_all | solution.py:120
  68.7 72.4 %all-gather.18.cloned.1.call-start = ((), (), s32[]{:S(2)}) async-start(), calls=%async_computation.8 | async-start | bytes 1622016 | tf_op jit(solution)/shard_map/all_gather | solution.py:138
  79.2 130.2 %all-gather.12.cloned.1.call-start = ((), (), s32[]{:S(2)}) async-start(), calls=%async_computation.5 | async-start | bytes 3244032 | tf_op jit(solution)/shard_map/all_gather | solution.py:111
  79.6 65.1 %copy-start.7 = (bf16[1,1,16,6144]{3,2,1,0:T(8,128)(2,1)S(1)}, bf16[1,1,16,6144]{3,2,1,0:T(8,128)(2,1)}, u32[]{:S(2)}) copy-start(bf16[1,1,16,6144]{3,2,1,0:T(8,128)(2,1)} %param.32) | copy-start | bytes 589828
  81.0 204.8 %all-gather.10.cloned.1.call-start = ((), (), s32[]{:S(2)}) async-start(), calls=%async_computation.4 | async-start | bytes 6488064 | tf_op jit(solution)/shard_map/all_gather | solution.py:149
  213.8 23.1 %all-to-all-start.1 = ((bf16[32,16,288]{2,1,0:T(8,128)(2,1)}), bf16[32,16,288]{2,1,0:T(8,128)(2,1)S(1)}, u32[]{:S(2)}, u32[]{:S(2)}) async-start(bf16[32,16,288]{2,1,0:T(8,128)(2,1)} %bitcast.21), calls=%async_computation.1 | async-start | bytes 786432 | tf_op jit(solution)/shard_map/all_to_all | solution.py:121
  220.4 136.3 %all-gather.14.cloned.1.call-start = ((), (), s32[]{:S(2)}) async-start(), calls=%async_computation.6 | async-start | bytes 6488064 | tf_op jit(solution)/shard_map/all_gather | solution.py:153
  239.0 236.0 %all-gather.16.cloned.1.call-start = ((), (), s32[]{:S(2)}) async-start(), calls=%async_computation.7 | async-start | bytes 3244032 | tf_op jit(solution)/shard_map/all_gather | solution.py:159
  372.0 3.5 copy-start.1
  375.5 1.9 copy-start.2
  379.2 315.3 %all-reduce.3.cloned.1.call-start = ((), (), s32[]{:S(2)}) async-start(), calls=%async_computation.9 | async-start | bytes 3145728
  413.9 15.0 %copy-start.6 = (bf16[1,1,4,3072]{3,2,1,0:T(4,128)(2,1)S(1)}, bf16[1,1,4,3072]{3,2,1,0:T(4,128)(2,1)}, u32[]{:S(2)}) copy-start(bf16[1,1,4,3072]{3,2,1,0:T(4,128)(2,1)} %param.18) | copy-start | bytes 73732
  413.9 15.0 %copy-start.12 = (f32[1,1,3072]{2,1,0:T(1,128)S(1)}, f32[1,1,3072]{2,1,0:T(1,128)}, u32[]{:S(2)}) copy-start(f32[1,1,3072]{2,1,0:T(1,128)} %get-tuple-element.27) | copy-start | bytes 36868
  413.9 15.4 %copy-start.10 = (f32[1,1,3072]{2,1,0:T(1,128)S(1)}, f32[1,1,3072]{2,1,0:T(1,128)}, u32[]{:S(2)}) copy-start(f32[1,1,3072]{2,1,0:T(1,128)} %get-tuple-element.23) | copy-start | bytes 36868
  413.9 15.4 %copy-start.11 = (f32[1,1,3072]{2,1,0:T(1,128)S(1)}, f32[1,1,3072]{2,1,0:T(1,128)}, u32[]{:S(2)}) copy-start(f32[1,1,3072]{2,1,0:T(1,128)} %get-tuple-element.24) | copy-start | bytes 36868
  467.6 5.4 copy-start.18
  467.6 7.3 %copy-start.14 = (bf16[4,6144]{1,0:T(4,128)(2,1)S(1)}, bf16[4,6144]{1,0:T(4,128)(2,1)}, u32[]{:S(2)}) copy-start(bf16[4,6144]{1,0:T(4,128)(2,1)} %param.33) | copy-start | bytes 147460
  471.6 3.4 copy-start.5
  475.0 219.6 %copy-start.9 = (f32[1,1,3072]{2,1,0:T(1,128)S(1)}, f32[1,1,3072]{2,1,0:T(1,128)}, u32[]{:S(2)}) copy-start(f32[1,1,3072]{2,1,0:T(1,128)} %get-tuple-element.22) | copy-start | bytes 36868
  478.0 217.7 %copy-start.4 = (bf16[1,1,16,3072]{3,2,1,0:T(8,128)(2,1)S(1)}, bf16[1,1,16,3072]{3,2,1,0:T(8,128)(2,1)}, u32[]{:S(2)}) copy-start(bf16[1,1,16,3072]{3,2,1,0:T(8,128)(2,1)} %param.19) | copy-start | bytes 294916
  478.0 217.7 %copy-start.8 = (f32[1,1,3072]{2,1,0:T(1,128)S(1)}, f32[1,1,3072]{2,1,0:T(1,128)}, u32[]{:S(2)}) copy-start(f32[1,1,3072]{2,1,0:T(1,128)} %get-tuple-element.32) | copy-start | bytes 36868
  478.0 224.8 %copy-start.16 = (bf16[3072,32]{0,1:T(8,128)(2,1)S(1)}, bf16[3072,32]{0,1:T(8,128)(2,1)}, u32[]{:S(2)}) copy-start(bf16[3072,32]{0,1:T(8,128)(2,1)} %param.34) | copy-start | bytes 589828
  478.0 224.8 %copy-start.17 = (f32[1,4,32]{2,1,0:T(4,128)S(1)}, f32[1,4,32]{2,1,0:T(4,128)}, u32[]{:S(2)}) copy-start(f32[1,4,32]{2,1,0:T(4,128)} %param.35) | copy-start | bytes 1540
  478.8 216.6 %all-to-all-start.3 = ((bf16[32,16,96]{2,1,0:T(8,128)(2,1)}), bf16[32,16,96]{2,1,0:T(8,128)(2,1)S(1)}, u32[]{:S(2)}, u32[]{:S(2)}) async-start(bf16[32,16,96]{2,1,0:T(8,128)(2,1)} %bitcast.47), calls=%async_computation.3 | async-start | bytes 262144 | tf_op jit(solution)/shard_map/all_to_all | solution.py:169
  695.8 6.6 collective-permute-start
Sparse Core Ops, SparseCore 0:
  79.3 61.7 all-gather.17
  143.5 65.7 all-gather.11
  211.8 74.0 all-gather.9
  287.5 69.1 all-gather.13
  379.3 66.5 all-gather.15
  471.8 222.6 all-reduce.2
where the time goes:
time: 713 us; the launch traced here: 712 us
  waiting for transfers between devices  462 us (65%)
  blocking collectives  124 us (17%)
  local copies, waits for them, and re-layouts  49.3 us (7%)
  between operations  24.4 us (3%)
  matrix products  22.6 us (3%)
  starting transfers between devices  16.9 us (2%)
  other arithmetic  13 us (2%)
    unnamed x7, waiting for transfers between devices  212 us
    all_gather x1, waiting for transfers between devices, shards(): lax.all_gather(text_normed, 'tok', axis=0, tiled=True)  62.8 us
    all_gather x1, waiting for transfers between devices, shards(): patch_rows = lax.all_gather(fresh_image, 'tok', axis=0, tiled=True)  59.4 us
    all_gather x1, waiting for transfers between devices, shards(): piece = lax.all_gather(fresh_text, 'tok', axis=0, tiled=True)  53 us
    all_gather x1, waiting for transfers between devices, shards(): piece = lax.all_gather(current, 'tok', axis=0, tiled=True)  45.5 us
    all_gather x1, blocking collectives, shards(): lax.all_gather(image_normed, 'tok', axis=0, tiled=True)  40.7 us
    all_gather x1, blocking collectives, shards(): lax.all_gather(mlp_normed, 'tok', axis=0, tiled=True)  36.7 us
    all_gather x1, blocking collectives, shards(): lax.all_gather(attended[:image_rows], 'tok', axis=0, tiled=True)  34.4 us
  transfers between devices with their start and end apart: 10, of which 8 were waited for; matrix products, arithmetic and copies ran while one was open for 6% of the time, Pallas kernels for 0%

commit v1 on v0

--- a/solution.py
+++ b/solution.py
@@ -155,7 +155,10 @@
     highest, total, mixed = attend(carry, queries, piece, where_text < text_count)
     attended = (mixed / total[..., None]).reshape(query_rows, width).astype(jnp.bfloat16)
     every_image_att, every_text_att = (
-        lax.all_gather(attended[:image_rows], "tok", axis=0, tiled=True),
+        jnp.concatenate(
+            lax.all_to_all(jnp.stack([attended[:image_rows]] * lax.axis_size("tok")), "tok", 0, 0),
+            axis=0,
+        ),
         lax.all_gather(attended[image_rows:], "tok", axis=0, tiled=True),
     )
     image_back_cols = jnp.dot(

time: 713 us -> 713 us (level)
    all_gather x1 -> x0, blocking collectives: 34.4 us -> none  [shards(): lax.all_gather(attended[:image_rows], 'tok', axis=0, tiled=True)]
    all_to_all x0 -> x1, blocking collectives: none -> 31.3 us  [shards(): lax.all_to_all(jnp.stack([attended[:image_rows]] * lax.axis_size('tok')),...]
    unnamed x50 -> x48, local copies, waits for them, and re-layouts: 18.7 us -> 17.6 us
where the time goes in v1:
time: 713 us; the launch traced here: 711 us
  waiting for transfers between devices  462 us (65%)
  blocking collectives  123 us (17%)
  local copies, waits for them, and re-layouts  49.5 us (7%)
  between operations  24.4 us (3%)
  matrix products  22.6 us (3%)
  starting transfers between devices  16.9 us (2%)
  other arithmetic  13 us (2%)
    unnamed x7, waiting for transfers between devices  213 us
    all_gather x1, waiting for transfers between devices, shards(): lax.all_gather(text_normed, 'tok', axis=0, tiled=True)  62.8 us
    all_gather x1, waiting for transfers between devices, shards(): patch_rows = lax.all_gather(fresh_image, 'tok', axis=0, tiled=True)  59.4 us
    all_gather x1, waiting for transfers between devices, shards(): piece = lax.all_gather(fresh_text, 'tok', axis=0, tiled=True)  53 us
    all_gather x1, waiting for transfers between devices, shards(): piece = lax.all_gather(current, 'tok', axis=0, tiled=True)  45.5 us
    all_gather x1, blocking collectives, shards(): lax.all_gather(image_normed, 'tok', axis=0, tiled=True)  40.7 us
    all_gather x1, blocking collectives, shards(): lax.all_gather(mlp_normed, 'tok', axis=0, tiled=True)  36.6 us
    all_to_all x1, blocking collectives, shards(): lax.all_to_all(jnp.stack([attended[:image_rows]] * lax.axis_size('tok')),...  31.3 us
  transfers between devices with their start and end apart: 10, of which 8 were waited for; matrix products, arithmetic and copies ran while one was open for 6% of the time, Pallas kernels for 0%

profile of v1, /device:TPU:1, one launch (start us, length us, event | category | flops | bytes accessed | tf_op | source)
XLA Modules:
  0.0 711.4 jit_solution(941385080455554234)
XLA Ops:
  7.2 1.5 fusion.114
  12.5 1.3 constant_dynamic-slice_fusion
  15.8 1.0 dynamic-slice_convert_fusion
  16.8 0.6 fusion.112
  17.4 0.9 convert_reduce_fusion.2
  18.3 0.9 fusion.80
  19.2 0.8 fusion.94
  20.1 40.7 %all-gather = bf16[32,4,3072]{2,1,0:T(4,128)(2,1)S(1)} all-gather(bf16[1,4,3072]{2,1,0:T(4,128)(2,1)S(1)} %fusion.94), channel_id=1, replica_groups=mesh['section'=2,'grp'=4,'tok'=32] {'tok'}, dimensions={0}, use_global_device_ids=true | all-gather | bytes 811008 | tf_op jit(solution)/shard_map/all_gather | solution.py:110
  60.8 1.1 reshape.270
  61.9 2.4 fusion.19
  64.4 0.7 all_to_all.51
  65.1 3.7 all-to-all-start
  68.8 8.5 %all-to-all-done = bf16[32,4,288]{2,1,0:T(4,128)(2,1)S(1)} async-done(((bf16[32,4,288]{2,1,0:T(4,128)(2,1)}), bf16[32,4,288]{2,1,0:T(4,128)(2,1)S(1)}, u32[]{:S(2)}, u32[]{:S(2)}) %all-to-all-start) | async-done | bytes 73760 | tf_op jit(solution)/shard_map/all_to_all | solution.py:120
  77.8 0.7 fusion.93
  78.5 0.6 maximum_bitcast_fusion
  79.4 0.2 fusion.40
  79.6 0.6 fusion.113
  80.3 0.7 fusion.43
  81.7 59.4 %all-gather.17.cloned.1.call-done = bf16[32,4,6144]{2,1,0:T(4,128)(2,1)} async-done(((bf16[1,4,6144]{2,1,0:T(4,128)(2,1)}), bf16[32,4,6144]{2,1,0:T(4,128)(2,1)}) %all-gather.17.cloned.1.call-update) | async-done | bytes 1572880 | tf_op jit(solution)/shard_map/all_gather | solution.py:138
  141.1 3.7 reshape.272
  144.8 1.7 bitcast_select_fusion
  146.5 62.8 %all-gather.11.cloned.1.call-done = bf16[512,3072]{1,0:T(8,128)(2,1)} async-done(((bf16[16,3072]{1,0:T(8,128)(2,1)}), bf16[512,3072]{1,0:T(8,128)(2,1)}) %all-gather.11.cloned.1.call-update) | async-done | bytes 3145744 | tf_op jit(solution)/shard_map/all_gather | solution.py:111
  209.3 3.5 fusion.11
  212.9 0.9 copy.62
  213.8 6.6 all-to-all-start.1
  220.5 16.5 %all-to-all-done.1 = bf16[32,16,288]{2,1,0:T(8,128)(2,1)S(1)} async-done(((bf16[32,16,288]{2,1,0:T(8,128)(2,1)}), bf16[32,16,288]{2,1,0:T(8,128)(2,1)S(1)}, u32[]{:S(2)}, u32[]{:S(2)}) %all-to-all-start.1) | async-done | bytes 294944 | tf_op jit(solution)/shard_map/all_to_all | solution.py:121
  237.0 0.5 all_to_all.58
  238.3 0.7 pad_maximum_fusion
  239.7 0.7 copy.105
  240.4 45.5 %all-gather.9.cloned.1.call-done = bf16[512,6144]{1,0:T(8,128)(2,1)} async-done(((bf16[16,6144]{1,0:T(8,128)(2,1)}), bf16[512,6144]{1,0:T(8,128)(2,1)}) %all-gather.9.cloned.1.call-update) | async-done | bytes 6291472 | tf_op jit(solution)/shard_map/all_gather | solution.py:149
  285.8 5.9 fusion.111
  291.7 4.8 copy.82
  296.5 4.7 copy.81
  301.2 2.6 fusion.115
  303.7 53.0 %all-gather.13.cloned.1.call-done = bf16[512,6144]{1,0:T(8,128)(2,1)} async-done(((bf16[16,6144]{1,0:T(8,128)(2,1)}), bf16[512,6144]{1,0:T(8,128)(2,1)}) %all-gather.13.cloned.1.call-update) | async-done | bytes 6291472 | tf_op jit(solution)/shard_map/all_gather | solution.py:153
  356.7 6.0 fusion.110
  362.7 4.7 copy.68
  367.4 4.7 copy.70
  372.0 2.7 fusion.116
  374.8 0.4 fusion.26
  375.1 0.4 fusion.24
  375.6 1.0 fusion.17
  376.5 0.9 copy-done.2
  377.4 1.0 fusion.18
  378.4 0.7 copy_bitcast_fusion
  379.2 0.2 all-reduce.3.cloned.1.call-start
  379.6 31.3 %all_to_all.69 = bf16[32,4,3072]{2,1,0:T(4,128)(2,1)S(1)} all-to-all(bf16[32,4,3072]{2,1,0:T(4,128)(2,1)S(1)} %stack.2), channel_id=1, replica_groups=mesh['section'=2,'grp'=4,'tok'=32] {'tok'}, dimensions={0} | all-to-all | bytes 1572864 | tf_op jit(solution)/shard_map/all_to_all | solution.py:159
  410.9 1.1 reshape.266
  412.0 1.7 convolution_convert_fusion.1
  413.8 14.0 %all_to_all.70 = bf16[32,4,96]{2,1,0:T(4,128)(2,1)S(1)} all-to-all(bf16[32,4,96]{2,1,0:T(4,128)(2,1)S(1)} %bitcast.220), channel_id=1, replica_groups=mesh['section'=2,'grp'=4,'tok'=32] {'tok'}, dimensions={0} | all-to-all | bytes 49152 | tf_op jit(solution)/shard_map/all_to_all | solution.py:171
  428.4 36.6 %all-gather.2 = bf16[32,4,3072]{2,1,0:T(4,128)(2,1)} all-gather(bf16[1,4,3072]{2,1,0:T(4,128)(2,1)S(1)} %fusion.92), channel_id=1, replica_groups=mesh['section'=2,'grp'=4,'tok'=32] {'tok'}, dimensions={0}, use_global_device_ids=true | all-gather | bytes 811008 | tf_op jit(solution)/shard_map/all_gather | solution.py:181
  465.0 1.6 reshape.274
  466.6 4.0 fusion
  472.0 0.6 dynamic-slice.5
  474.0 3.0 convolution_convert_fusion
  477.1 0.8 copy.75
  477.8 3.7 all-to-all-start.4
  481.5 212.6 %all-reduce.3.cloned.1.call-done = f32[128,3072]{1,0:T(8,128)} async-done(((f32[128,3072]{1,0:T(8,128)}), f32[128,3072]{1,0:T(8,128)}) %all-reduce.3.cloned.1.call-update) | async-done | bytes 1572880
  694.1 0.9 fusion.91
  695.4 2.5 collective-permute-start
  697.9 4.1 collective-permute-done
  702.4 0.8 fusion.23
  703.2 0.6 slice_bitcast_fusion.3
  703.8 0.7 slice_bitcast_fusion
  (106 shorter events, 3.7 us)
Async XLA Ops:
  7.2 459.4 %copy-start = (bf16[1,384,3072]{2,1,0:T(8,128)(2,1)S(1)}, bf16[1,384,3072]{2,1,0:T(8,128)(2,1)}, u32[]{:S(2)}) copy-start(bf16[1,384,3072]{2,1,0:T(8,128)(2,1)} %param.31) | copy-start | bytes 7077892
  61.9 6.9 copy-start.15
  61.9 17.3 %copy-start.3 = (bf16[1,1,16,3072]{3,2,1,0:T(8,128)(2,1)S(1)}, bf16[1,1,16,3072]{3,2,1,0:T(8,128)(2,1)}, u32[]{:S(2)}) copy-start(bf16[1,1,16,3072]{3,2,1,0:T(8,128)(2,1)} %param.19) | copy-start | bytes 294916
  61.9 17.7 %copy-start.13 = (bf16[1,4,9216]{2,1,0:T(4,128)(2,1)S(1)}, bf16[1,4,9216]{2,1,0:T(4,128)(2,1)}, u32[]{:S(2)}) copy-start(bf16[1,4,9216]{2,1,0:T(4,128)(2,1)} %param.24) | copy-start | bytes 221188
  65.1 12.2 %all-to-all-start = ((bf16[32,4,288]{2,1,0:T(4,128)(2,1)}), bf16[32,4,288]{2,1,0:T(4,128)(2,1)S(1)}, u32[]{:S(2)}, u32[]{:S(2)}) async-start(bf16[32,4,288]{2,1,0:T(4,128)(2,1)} %all_to_all.51), calls=%async_computation | async-start | bytes 196608 | tf_op jit(solution)/shard_map/all_to_all | solution.py:120
  68.7 72.4 %all-gather.17.cloned.1.call-start = ((), (), s32[]{:S(2)}) async-start(), calls=%async_computation.9 | async-start | bytes 1622016 | tf_op jit(solution)/shard_map/all_gather | solution.py:138
  79.2 130.2 %all-gather.11.cloned.1.call-start = ((), (), s32[]{:S(2)}) async-start(), calls=%async_computation.6 | async-start | bytes 3244032 | tf_op jit(solution)/shard_map/all_gather | solution.py:111
  79.6 65.1 %copy-start.7 = (bf16[1,1,16,6144]{3,2,1,0:T(8,128)(2,1)S(1)}, bf16[1,1,16,6144]{3,2,1,0:T(8,128)(2,1)}, u32[]{:S(2)}) copy-start(bf16[1,1,16,6144]{3,2,1,0:T(8,128)(2,1)} %param.32) | copy-start | bytes 589828
  81.0 204.8 %all-gather.9.cloned.1.call-start = ((), (), s32[]{:S(2)}) async-start(), calls=%async_computation.5 | async-start | bytes 6488064 | tf_op jit(solution)/shard_map/all_gather | solution.py:149
  213.8 23.1 %all-to-all-start.1 = ((bf16[32,16,288]{2,1,0:T(8,128)(2,1)}), bf16[32,16,288]{2,1,0:T(8,128)(2,1)S(1)}, u32[]{:S(2)}, u32[]{:S(2)}) async-start(bf16[32,16,288]{2,1,0:T(8,128)(2,1)} %bitcast.21), calls=%async_computation.1 | async-start | bytes 786432 | tf_op jit(solution)/shard_map/all_to_all | solution.py:121
  220.4 136.3 %all-gather.13.cloned.1.call-start = ((), (), s32[]{:S(2)}) async-start(), calls=%async_computation.7 | async-start | bytes 6488064 | tf_op jit(solution)/shard_map/all_gather | solution.py:153
  239.0 235.0 %all-gather.15.cloned.1.call-start = ((), (), s32[]{:S(2)}) async-start(), calls=%async_computation.8 | async-start | bytes 3244032 | tf_op jit(solution)/shard_map/all_gather | solution.py:162
  372.0 3.5 copy-start.1
  375.5 1.9 copy-start.2
  379.2 314.9 %all-reduce.3.cloned.1.call-start = ((), (), s32[]{:S(2)}) async-start(), calls=%async_computation.10 | async-start | bytes 3145728
  410.9 17.0 %copy-start.6 = (bf16[1,1,4,3072]{3,2,1,0:T(4,128)(2,1)S(1)}, bf16[1,1,4,3072]{3,2,1,0:T(4,128)(2,1)}, u32[]{:S(2)}) copy-start(bf16[1,1,4,3072]{3,2,1,0:T(4,128)(2,1)} %param.18) | copy-start | bytes 73732
  410.9 17.0 %copy-start.12 = (f32[1,1,3072]{2,1,0:T(1,128)S(1)}, f32[1,1,3072]{2,1,0:T(1,128)}, u32[]{:S(2)}) copy-start(f32[1,1,3072]{2,1,0:T(1,128)} %get-tuple-element.27) | copy-start | bytes 36868
  410.9 17.4 %copy-start.10 = (f32[1,1,3072]{2,1,0:T(1,128)S(1)}, f32[1,1,3072]{2,1,0:T(1,128)}, u32[]{:S(2)}) copy-start(f32[1,1,3072]{2,1,0:T(1,128)} %get-tuple-element.23) | copy-start | bytes 36868
  410.9 17.4 %copy-start.11 = (f32[1,1,3072]{2,1,0:T(1,128)S(1)}, f32[1,1,3072]{2,1,0:T(1,128)}, u32[]{:S(2)}) copy-start(f32[1,1,3072]{2,1,0:T(1,128)} %get-tuple-element.24) | copy-start | bytes 36868
  466.6 5.4 copy-start.18
  466.6 7.3 %copy-start.14 = (bf16[4,6144]{1,0:T(4,128)(2,1)S(1)}, bf16[4,6144]{1,0:T(4,128)(2,1)}, u32[]{:S(2)}) copy-start(bf16[4,6144]{1,0:T(4,128)(2,1)} %param.33) | copy-start | bytes 147460
  470.7 3.4 copy-start.5
  474.0 220.1 %copy-start.9 = (f32[1,1,3072]{2,1,0:T(1,128)S(1)}, f32[1,1,3072]{2,1,0:T(1,128)}, u32[]{:S(2)}) copy-start(f32[1,1,3072]{2,1,0:T(1,128)} %get-tuple-element.22) | copy-start | bytes 36868
  477.0 218.3 %copy-start.4 = (bf16[1,1,16,3072]{3,2,1,0:T(8,128)(2,1)S(1)}, bf16[1,1,16,3072]{3,2,1,0:T(8,128)(2,1)}, u32[]{:S(2)}) copy-start(bf16[1,1,16,3072]{3,2,1,0:T(8,128)(2,1)} %param.19) | copy-start | bytes 294916
  477.0 218.3 %copy-start.8 = (f32[1,1,3072]{2,1,0:T(1,128)S(1)}, f32[1,1,3072]{2,1,0:T(1,128)}, u32[]{:S(2)}) copy-start(f32[1,1,3072]{2,1,0:T(1,128)} %get-tuple-element.32) | copy-start | bytes 36868
  477.0 225.4 %copy-start.16 = (bf16[3072,32]{0,1:T(8,128)(2,1)S(1)}, bf16[3072,32]{0,1:T(8,128)(2,1)}, u32[]{:S(2)}) copy-start(bf16[3072,32]{0,1:T(8,128)(2,1)} %param.34) | copy-start | bytes 589828
  477.0 225.4 %copy-start.17 = (f32[1,4,32]{2,1,0:T(4,128)S(1)}, f32[1,4,32]{2,1,0:T(4,128)}, u32[]{:S(2)}) copy-start(f32[1,4,32]{2,1,0:T(4,128)} %param.35) | copy-start | bytes 1540
  477.8 217.2 %all-to-all-start.4 = ((bf16[32,16,96]{2,1,0:T(8,128)(2,1)}), bf16[32,16,96]{2,1,0:T(8,128)(2,1)S(1)}, u32[]{:S(2)}, u32[]{:S(2)}) async-start(bf16[32,16,96]{2,1,0:T(8,128)(2,1)} %bitcast.47), calls=%async_computation.4 | async-start | bytes 262144 | tf_op jit(solution)/shard_map/all_to_all | solution.py:172
  695.4 6.6 collective-permute-start
Sparse Core Ops, SparseCore 0:
  79.3 61.7 all-gather.16
  143.5 65.7 all-gather.10
  211.8 74.0 all-gather.8
  287.5 69.1 all-gather.12
  379.3 70.2 all-gather.14
  470.8 223.2 all-reduce.2
